TPU v7x, 32 devices: a whole 2x2x4 slice. The times are simulated.
32 devices in a mesh: rep: 2 (over y), seq: 4 (over z), head: 4 (over x, core).
Axes of the slice: x: 2, y: 2, z: 4, core: 2. Of those that a mesh axis runs over, the one named last changes fastest.
Arguments:
- queries: bfloat16 [3072, 2560], P(('rep', 'seq'), 'head'), parts along dimension 0, may hold values from -16 to 16
- keys: bfloat16 [3072, 2560], P(('rep', 'seq'), 'head'), parts along dimension 0, may hold values from -6 to 6
- values: bfloat16 [3072, 2560], P(('rep', 'seq'), 'head'), parts along dimension 0, may hold values from -6 to 6
- out_weight: bfloat16 [2560, 5120], P('seq', 'head'), may hold values from -0.3125 to 0.3125
- neighbours: int32 [8, 27], P('rep'), parts along dimension 0, may hold values from -1 to 3, as said below
- clip_ids: int32 [3072], P(('rep', 'seq')), parts along dimension 0, may hold values from 0 to 1
Outputs:
- output: bfloat16 [3072, 5120], P(('rep', 'seq'), 'head'), parts along dimension 0
There are 2 independent parts, one for each index of `rep`. A program takes and returns all parts, laid end to end along the dimension named above; an argument that names none is the same for every part. Nothing has to cross between parts.
Inputs may be any that keep to these rules, and one draw needn't show every extreme that they name: `neighbours`: column 9 (a + 1) + 3 (b + 1) + (c + 1) of row s, for a, b, c each -1, 0 or 1, is either -1 or s + a * 4 * 7 + b * 7 + c; column 13 of row s is s.
All inputs are finite; a program needn't handle non-finite values.
Results may differ from a plain program's by a relative error of at most 0.0058.
Values may be sent and summed in bfloat16 or wider, within the bound.
No kernel may reach another device: no remote copies, remote signals or barrier semaphores. Data moves between devices by JAX's collectives and lax.ppermute only.
A program may use at most 192 MiB of HBM per device.

v0:
```python
import math
import jax
import jax.numpy as jnp
from jax import lax
from jax.sharding import PartitionSpec as P

HD = 128
TGH = 4
TGW = 7


def from_behind(value, axis, by):
    peers = lax.axis_size(axis)
    pairs = [(i, i + by) for i in range(peers) if 0 <= i + by < peers]
    return lax.ppermute(value, axis, pairs)


def attend_head(query_head, key_head, value_head, allowed):
    scores = lax.dot_general(
        query_head, key_head, (((1,), (1,)), ((), ())), preferred_element_type=jnp.float32
    ) * (1.0 / math.sqrt(query_head.shape[1]))
    masked = jnp.where(allowed, scores, -1e30)
    highest = jnp.max(masked, axis=1, keepdims=True)
    raised = jnp.where(allowed, jnp.exp(masked - highest), 0.0)
    summed = jnp.sum(raised, axis=1, keepdims=True)
    weights = (raised / summed).astype(jnp.bfloat16)
    return jnp.dot(weights, value_head, preferred_element_type=jnp.float32).astype(jnp.bfloat16)


def on_device(queries, keys, values, out_weight, neighbours, clip_ids):
    tile_rows = queries.shape[0]
    feature_width = queries.shape[1]
    seq_count = lax.axis_size("seq")
    layer_tiles = TGH * TGW
    every_offset = set()
    for layer_step in (-1, 0, 1):
        for row_step in (-1, 0, 1):
            for col_step in (-1, 0, 1):
                every_offset.add(layer_step * layer_tiles + row_step * TGW + col_step)
    distances = [offset for offset in sorted(every_offset) if 0 < offset < seq_count]
    key_list = [keys]
    value_list = [values]
    clip_list = [clip_ids]
    offsets = [0]
    for distance in distances:
        below_keys, below_values, below_clips = from_behind(
            (keys, values, clip_ids), "seq", distance
        )
        above_keys, above_values, above_clips = from_behind(
            (keys, values, clip_ids), "seq", -distance
        )
        key_list += [below_keys, above_keys]
        value_list += [below_values, above_values]
        clip_list += [below_clips, above_clips]
        offsets += [distance, -distance]
    key_stack = jnp.stack(key_list)
    value_stack = jnp.stack(value_list)
    clip_stack = jnp.stack(clip_list)
    blocks = key_stack.shape[0]
    position = lax.axis_index("seq")
    window_row = lax.dynamic_index_in_dim(neighbours, position, 0, keepdims=False)
    sources = position - jnp.asarray(offsets, dtype=jnp.int32)
    present = jnp.any(
        (window_row[None, :] == sources[:, None]) & (window_row[None, :] >= 0), axis=1
    )
    key_clips = clip_stack.reshape(blocks * tile_rows)
    allowed = jnp.repeat(present, tile_rows)[None, :] & (clip_ids[:, None] == key_clips[None, :])
    key_rows = key_stack.reshape(blocks * tile_rows, feature_width)
    value_rows = value_stack.reshape(blocks * tile_rows, feature_width)
    head_outputs = []
    for head_index in range(feature_width // HD):
        first_col = head_index * HD
        head_outputs.append(
            attend_head(
                queries[:, first_col : first_col + HD],
                key_rows[:, first_col : first_col + HD],
                value_rows[:, first_col : first_col + HD],
                allowed,
            )
        )
    attended = jnp.concatenate(head_outputs, axis=1)
    all_features = lax.all_gather(attended, "head", axis=1, tiled=True)
    empty = jnp.zeros((tile_rows, out_weight.shape[1]), jnp.float32)
    weight_piece = lax.all_gather(out_weight, "seq", axis=0, tiled=True)
    features = lax.slice_in_dim(all_features, 0, weight_piece.shape[0], axis=1)
    projected = empty + jnp.dot(features, weight_piece, preferred_element_type=jnp.float32)
    return projected.astype(jnp.bfloat16)


def solution(mesh):
    in_specs = (
        P(("rep", "seq"), "head"),
        P(("rep", "seq"), "head"),
        P(("rep", "seq"), "head"),
        P("seq", "head"),
        P("rep", None),
        P(("rep", "seq")),
    )
    out_specs = P(("rep", "seq"), "head")
    return jax.shard_map(
        on_device, mesh=mesh, in_specs=in_specs, out_specs=out_specs, check_vma=False
    )
```

profile of v0, /device:TPU:0, one launch (start us, length us, event | category | flops | bytes accessed | tf_op | source)
XLA Modules:
  0.0 208.0 jit_solution(14518805611755408136)
XLA Ops:
  6.5 0.0 copy-start.2
  6.5 0.0 copy-start.3
  6.5 0.0 all-gather.3.cloned.1.call-start
  6.5 5.0 %collective-permute-start = (s32[384]{0:T(512)}, s32[384]{0:T(512)S(1)}, u32[]{:S(2)}, u32[]{:S(2)}) collective-permute-start(s32[384]{0:T(512)} %param.12), channel_id=1, source_target_pairs={{0,4},{4,8},{8,12},{1,5},{5,9},{9,13},{2,6},{6,10},{10,14},{3,7},{... | collective-permute-start | bytes 4616 | tf_op jit(solution)/shard_map/ppermute | solution.py:15
  11.6 1.3 collective-permute-start.1
  12.9 4.6 %collective-permute-start.2 = (bf16[384,640]{1,0:T(8,128)(2,1)}, bf16[384,640]{1,0:T(8,128)(2,1)S(1)}, u32[]{:S(2)}, u32[]{:S(2)}) collective-permute-start(bf16[384,640]{1,0:T(8,128)(2,1)} %param.8), channel_id=1, source_target_pairs={{0,4},{4,8},{8,12},{1,5},{5,9},{9,13},{2,6},{6,10},{10,14},{3,7},{... | collective-permute-start | bytes 1474568 | tf_op jit(solution)/shard_map/ppermute | solution.py:15
  17.5 1.3 collective-permute-start.3
  18.8 4.6 %collective-permute-start.4 = (bf16[384,640]{1,0:T(8,128)(2,1)}, bf16[384,640]{1,0:T(8,128)(2,1)S(1)}, u32[]{:S(2)}, u32[]{:S(2)}) collective-permute-start(bf16[384,640]{1,0:T(8,128)(2,1)} %param.9), channel_id=1, source_target_pairs={{0,4},{4,8},{8,12},{1,5},{5,9},{9,13},{2,6},{6,10},{10,14},{3,7},{... | collective-permute-start | bytes 1474568 | tf_op jit(solution)/shard_map/ppermute | solution.py:15
  23.4 0.7 compare_bitcast_fusion
  24.1 0.7 fusion.35
  24.8 0.7 broadcast_add_fusion
  25.4 0.2 and_reduce_fusion
  25.6 0.7 stack.36
  26.3 0.1 broadcast_in_dim.32
  26.4 0.0 collective-permute-done
  26.4 1.3 collective-permute-start.5
  27.7 0.0 collective-permute-done.1
  27.8 1.7 collective-permute-done.2
  29.4 4.3 %collective-permute-done.3 = bf16[384,640]{1,0:T(8,128)(2,1)S(1)} collective-permute-done((bf16[384,640]{1,0:T(8,128)(2,1)}, bf16[384,640]{1,0:T(8,128)(2,1)S(1)}, u32[]{:S(2)}, u32[]{:S(2)}) %collective-permute-start.3) | collective-permute-done | bytes 491552 | tf_op jit(solution)/shard_map/ppermute | solution.py:15
  33.8 1.2 pad_maximum_fusion
  35.0 0.0 copy-done.2
  35.0 0.0 copy-done.3
  35.0 0.6 fusion.41
  35.6 0.6 fusion.42
  36.3 0.6 fusion.43
  36.9 0.6 fusion.44
  37.5 0.0 copy-start
  37.5 0.6 fusion.45
  38.2 0.1 collective-permute-done.4
  38.2 4.0 %collective-permute-done.5 = bf16[384,640]{1,0:T(8,128)(2,1)S(1)} collective-permute-done((bf16[384,640]{1,0:T(8,128)(2,1)}, bf16[384,640]{1,0:T(8,128)(2,1)S(1)}, u32[]{:S(2)}, u32[]{:S(2)}) %collective-permute-start.5) | collective-permute-done | bytes 491552 | tf_op jit(solution)/shard_map/ppermute | solution.py:15
  42.2 0.0 copy-done
  42.3 0.2 pad_maximum_fusion.1
  42.4 2.3 %fusion.14 = (f32[384]{0:T(512)S(1)}, f32[384]{0:T(512)S(1)}, f32[384]{0:T(512)S(1)}, f32[384]{0:T(512)S(1)}, f32[384]{0:T(512)S(1)}) fusion(f32[384,1152]{0,1:T(8,128)S(1)} %get-tuple-element.11, f32[384]{0:T(512)S(1)} %get-tuple-element.10, s32[384]{0:T(512)S(1)} %copy-done.2, s32[1152]{0:T(1024)S(1)} %eq.35, pred[1152]{0:T(1024)(128)(4,1)S(1)} %and.24, ...), kind=kLoop, calls=%fused_computation.33 | loop fusion | flops 7518336 | bytes 8870016 | tf_op jit(solution)/shard_map/reduce_sum | solution.py:25
  44.7 1.0 fusion.15
  45.7 1.0 fusion.16
  46.8 1.0 fusion.17
  47.8 1.0 fusion.18
  48.8 1.0 fusion.19
  49.8 0.0 copy-start.1
  49.8 0.8 copy-done.1
  50.6 0.0 all-gather.3.cloned.1.call-update
  50.6 0.0 all-gather.5.cloned.1.call-start
  50.7 0.7 all-gather.5.cloned.1.call-update
  51.4 21.5 %all-gather.3.cloned.1.call-done = bf16[384,2560]{1,0:T(8,128)(2,1)} async-done(((bf16[384,640]{1,0:T(8,128)(2,1)}), bf16[384,2560]{1,0:T(8,128)(2,1)}) %all-gather.3.cloned.1.call-update) | async-done | bytes 1966096 | tf_op jit(solution)/shard_map/all_gather | solution.py:82
  72.8 121.2 %all-gather.5.cloned.1.call-done = bf16[2560,1280]{1,0:T(8,128)(2,1)} async-done(((bf16[640,1280]{1,0:T(8,128)(2,1)}), bf16[2560,1280]{1,0:T(8,128)(2,1)}) %all-gather.5.cloned.1.call-update) | async-done | bytes 6553616 | tf_op jit(solution)/shard_map/all_gather | solution.py:84
  194.1 7.1 %convolution_convert_fusion = bf16[384,1280]{1,0:T(8,128)(2,1)} fusion(bf16[384,2560]{1,0:T(8,128)(2,1)} %all-gather.3.cloned.1.call-done, bf16[2560,1280]{1,0:T(8,128)(2,1)} %all-gather.5.cloned.1.call-done), kind=kOutput, calls=%fused_computation.15 | convolution fusion | flops 2517073920 | bytes 9502720 | tf_op jit(solution)/shard_map/dot_general | solution.py:86
  (5 shorter events, 0.0 us)
Async XLA Ops:
  6.5 28.4 %copy-start.2 = (s32[384]{0:T(512)S(1)}, s32[384]{0:T(512)}, u32[]{:S(2)}) copy-start(s32[384]{0:T(512)} %param.12) | copy-start | bytes 4612
  6.5 28.5 %copy-start.3 = (bf16[384,640]{1,0:T(8,128)(2,1)S(1)}, bf16[384,640]{1,0:T(8,128)(2,1)}, u32[]{:S(2)}) copy-start(bf16[384,640]{1,0:T(8,128)(2,1)} %param.7) | copy-start | bytes 1474564
  6.5 66.3 %all-gather.3.cloned.1.call-start = ((), (), s32[]{:S(2)}) async-start(), calls=%async_computation | async-start | bytes 2457600 | tf_op jit(solution)/shard_map/all_gather | solution.py:82
  6.5 19.8 %collective-permute-start = (s32[384]{0:T(512)}, s32[384]{0:T(512)S(1)}, u32[]{:S(2)}, u32[]{:S(2)}) collective-permute-start(s32[384]{0:T(512)} %param.12), channel_id=1, source_target_pairs={{0,4},{4,8},{8,12},{1,5},{5,9},{9,13},{2,6},{6,10},{10,14},{3,7},{... | collective-permute-start | bytes 4616 | tf_op jit(solution)/shard_map/ppermute | solution.py:15
  11.6 16.1 %collective-permute-start.1 = (s32[384]{0:T(512)}, s32[384]{0:T(512)S(1)}, u32[]{:S(2)}, u32[]{:S(2)}) collective-permute-start(s32[384]{0:T(512)} %param.12), channel_id=1, source_target_pairs={{4,0},{8,4},{12,8},{5,1},{9,5},{13,9},{6,2},{10,6},{14,10},{7,3},{... | collective-permute-start | bytes 4616 | tf_op jit(solution)/shard_map/ppermute | solution.py:15
  12.9 16.5 %collective-permute-start.2 = (bf16[384,640]{1,0:T(8,128)(2,1)}, bf16[384,640]{1,0:T(8,128)(2,1)S(1)}, u32[]{:S(2)}, u32[]{:S(2)}) collective-permute-start(bf16[384,640]{1,0:T(8,128)(2,1)} %param.8), channel_id=1, source_target_pairs={{0,4},{4,8},{8,12},{1,5},{5,9},{9,13},{2,6},{6,10},{10,14},{3,7},{... | collective-permute-start | bytes 1474568 | tf_op jit(solution)/shard_map/ppermute | solution.py:15
  17.5 16.3 %collective-permute-start.3 = (bf16[384,640]{1,0:T(8,128)(2,1)}, bf16[384,640]{1,0:T(8,128)(2,1)S(1)}, u32[]{:S(2)}, u32[]{:S(2)}) collective-permute-start(bf16[384,640]{1,0:T(8,128)(2,1)} %param.8), channel_id=1, source_target_pairs={{4,0},{8,4},{12,8},{5,1},{9,5},{13,9},{6,2},{10,6},{14,10},{7,3},{... | collective-permute-start | bytes 1474568 | tf_op jit(solution)/shard_map/ppermute | solution.py:15
  18.8 19.4 %collective-permute-start.4 = (bf16[384,640]{1,0:T(8,128)(2,1)}, bf16[384,640]{1,0:T(8,128)(2,1)S(1)}, u32[]{:S(2)}, u32[]{:S(2)}) collective-permute-start(bf16[384,640]{1,0:T(8,128)(2,1)} %param.9), channel_id=1, source_target_pairs={{0,4},{4,8},{8,12},{1,5},{5,9},{9,13},{2,6},{6,10},{10,14},{3,7},{... | collective-permute-start | bytes 1474568 | tf_op jit(solution)/shard_map/ppermute | solution.py:15
  26.4 15.9 %collective-permute-start.5 = (bf16[384,640]{1,0:T(8,128)(2,1)}, bf16[384,640]{1,0:T(8,128)(2,1)S(1)}, u32[]{:S(2)}, u32[]{:S(2)}) collective-permute-start(bf16[384,640]{1,0:T(8,128)(2,1)} %param.9), channel_id=1, source_target_pairs={{4,0},{8,4},{12,8},{5,1},{9,5},{13,9},{6,2},{10,6},{14,10},{7,3},{... | collective-permute-start | bytes 1474568 | tf_op jit(solution)/shard_map/ppermute | solution.py:15
  37.5 4.7 %copy-start = (bf16[384,640]{1,0:T(8,128)(2,1)S(1)}, bf16[384,640]{1,0:T(8,128)(2,1)}, u32[]{:S(2)}) copy-start(bf16[384,640]{1,0:T(8,128)(2,1)} %param.9) | copy-start | bytes 1474564
  49.8 0.8 copy-start.1
  50.6 143.4 %all-gather.5.cloned.1.call-start = ((), (), s32[]{:S(2)}) async-start(), calls=%async_computation.1 | async-start | bytes 8192000 | tf_op jit(solution)/shard_map/all_gather | solution.py:84
Sparse Core Ops, SparseCore 0:
  50.7 22.0 all-gather.2
  74.4 119.6 all-gather.4
where the time goes:
time: 208 us
  waiting for transfers between devices  154 us (74%)
  starting transfers between devices  18.1 us (9%)
  matrix products  15.3 us (7%)
  between operations  13.6 us (7%)
  other arithmetic  5.25 us (3%)
  local copies, waits for them, and re-layouts  2.27 us (1%)
    all_gather x1, waiting for transfers between devices, on_device(): weight_piece = lax.all_gather(out_weight, 'seq', axis=0, tiled=True)  121 us
    all_gather x1, waiting for transfers between devices, on_device(): all_features = lax.all_gather(attended, 'head', axis=1, tiled=True)  21.5 us
    ppermute x6, starting transfers between devices, from_behind(): return lax.ppermute(value, axis, pairs)  18.1 us
    ppermute x6, waiting for transfers between devices, from_behind(): return lax.ppermute(value, axis, pairs)  10.1 us
    dot_general x1, matrix products, on_device(): jnp.dot(features, weight_piece, preferred_element_type=jnp.float32)  7.1 us
    dot_general x5, matrix products, attend_head(): jnp.dot(weights, value_head, preferred_element_type=jnp.float32)  5.04 us
  transfers between devices with their start and end apart: 8, of which 6 were waited for; matrix products, arithmetic and copies ran while one was open for 4% of the time, Pallas kernels for 0%

commit v1 on v0

--- a/solution.py
+++ b/solution.py
@@ -79,7 +79,16 @@
             )
         )
     attended = jnp.concatenate(head_outputs, axis=1)
-    all_features = lax.all_gather(attended, "head", axis=1, tiled=True)
+    size_here = lax.axis_size("head")
+    passed = attended
+    front = sorted(((k, (k + 1) % size_here) for k in range(size_here)))
+    lanes = [passed]
+    for nth in range(1, size_here):
+        passed = lax.ppermute(passed, "head", front)
+        lanes.insert(0, passed)
+    piece_next = jnp.concatenate(lanes, axis=1)
+    y_new = lax.axis_index("head") + 1
+    all_features = jnp.roll(piece_next, y_new * attended.shape[1], axis=1)
     empty = jnp.zeros((tile_rows, out_weight.shape[1]), jnp.float32)
     weight_piece = lax.all_gather(out_weight, "seq", axis=0, tiled=True)
     features = lax.slice_in_dim(all_features, 0, weight_piece.shape[0], axis=1)

time: 208 us -> 159 us (0.76)
  waiting for transfers between devices: 154 us -> 94 us
  local copies, waits for them, and re-layouts: 2.27 us -> 13.8 us
    all_gather x1, waiting for transfers between devices: 121 us -> 28.9 us  [on_device(): weight_piece = lax.all_gather(out_weight, 'seq', axis=0, tiled=True)]
    ppermute x6, waiting for transfers between devices: 10.1 us -> 39.6 us  [from_behind(): return lax.ppermute(value, axis, pairs)]
    ppermute x0 -> x3, waiting for transfers between devices: none -> 24.7 us  [on_device(): passed = lax.ppermute(passed, 'head', front)]
    all_gather x1 -> x0, waiting for transfers between devices: 21.5 us -> none  [on_device(): all_features = lax.all_gather(attended, 'head', axis=1, tiled=True)]
    unnamed x8 -> x23, local copies, waits for them, and re-layouts: 0.79 us -> 11.7 us
  transfers between devices with their start and end apart: 8 -> 10, of which waited for: 6 -> 6; matrix products, arithmetic and copies ran while one was open for 4% -> 16% of each run, Pallas kernels for 0% -> 0%
where the time goes in v1:
time: 159 us
  waiting for transfers between devices  94 us (59%)
  starting transfers between devices  18.1 us (11%)
  matrix products  14.9 us (9%)
  local copies, waits for them, and re-layouts  13.8 us (9%)
  between operations  13.6 us (9%)
  other arithmetic  4.24 us (3%)
    ppermute x6, waiting for transfers between devices, from_behind(): return lax.ppermute(value, axis, pairs)  39.6 us
    all_gather x1, waiting for transfers between devices, on_device(): weight_piece = lax.all_gather(out_weight, 'seq', axis=0, tiled=True)  28.9 us
    ppermute x3, waiting for transfers between devices, on_device(): passed = lax.ppermute(passed, 'head', front)  24.7 us
    ppermute x6, starting transfers between devices, from_behind(): return lax.ppermute(value, axis, pairs)  18.1 us
    unnamed x23, local copies, waits for them, and re-layouts  11.7 us
    dot_general x1, matrix products, on_device(): jnp.dot(features, weight_piece, preferred_element_type=jnp.float32)  7.17 us
    dot_general x5, matrix products, attend_head(): jnp.dot(weights, value_head, preferred_element_type=jnp.float32)  4.62 us
  transfers between devices with their start and end apart: 10, of which 6 were waited for; matrix products, arithmetic and copies ran while one was open for 16% of the time, Pallas kernels for 0%

profile of v1, /device:TPU:0, one launch (start us, length us, event | category | flops | bytes accessed | tf_op | source)
XLA Modules:
  0.0 158.7 jit_solution(13809563600175920477)
XLA Ops:
  6.5 0.0 all-gather.2.cloned.1.call-start
  6.5 0.7 all-gather.2.cloned.1.call-update
  7.3 0.0 copy-start.1
  7.3 5.1 %collective-permute-start.2 = (bf16[384,640]{1,0:T(8,128)(2,1)}, bf16[384,640]{1,0:T(8,128)(2,1)S(1)}, u32[]{:S(2)}, u32[]{:S(2)}) collective-permute-start(bf16[384,640]{1,0:T(8,128)(2,1)} %param.8), channel_id=1, source_target_pairs={{0,4},{4,8},{8,12},{1,5},{5,9},{9,13},{2,6},{6,10},{10,14},{3,7},{... | collective-permute-start | bytes 1474568 | tf_op jit(solution)/shard_map/ppermute | solution.py:15
  12.4 1.3 collective-permute-start.3
  13.7 4.6 %collective-permute-start.4 = (bf16[384,640]{1,0:T(8,128)(2,1)}, bf16[384,640]{1,0:T(8,128)(2,1)S(1)}, u32[]{:S(2)}, u32[]{:S(2)}) collective-permute-start(bf16[384,640]{1,0:T(8,128)(2,1)} %param.9), channel_id=1, source_target_pairs={{0,4},{4,8},{8,12},{1,5},{5,9},{9,13},{2,6},{6,10},{10,14},{3,7},{... | collective-permute-start | bytes 1474568 | tf_op jit(solution)/shard_map/ppermute | solution.py:15
  18.2 1.3 collective-permute-start.5
  19.5 4.5 %collective-permute-start = (s32[384]{0:T(512)}, s32[384]{0:T(512)S(1)}, u32[]{:S(2)}, u32[]{:S(2)}) collective-permute-start(s32[384]{0:T(512)} %param.12), channel_id=1, source_target_pairs={{0,4},{4,8},{8,12},{1,5},{5,9},{9,13},{2,6},{6,10},{10,14},{3,7},{... | collective-permute-start | bytes 4616 | tf_op jit(solution)/shard_map/ppermute | solution.py:15
  24.1 0.7 broadcast_add_fusion
  24.8 0.7 compare_bitcast_fusion
  25.5 0.7 fusion.32
  26.1 21.0 %collective-permute-done = s32[384]{0:T(512)S(1)} collective-permute-done((s32[384]{0:T(512)}, s32[384]{0:T(512)S(1)}, u32[]{:S(2)}, u32[]{:S(2)}) %collective-permute-start) | collective-permute-done | bytes 1568 | tf_op jit(solution)/shard_map/ppermute | solution.py:15
  47.1 1.3 collective-permute-start.1
  48.4 0.2 and_reduce_fusion
  48.6 0.7 stack.36
  49.3 0.1 broadcast_in_dim.32
  49.4 18.6 %collective-permute-done.1 = s32[384]{0:T(512)S(1)} collective-permute-done((s32[384]{0:T(512)}, s32[384]{0:T(512)S(1)}, u32[]{:S(2)}, u32[]{:S(2)}) %collective-permute-start.1) | collective-permute-done | bytes 1568 | tf_op jit(solution)/shard_map/ppermute | solution.py:15
  68.0 0.0 collective-permute-done.2
  68.0 0.0 collective-permute-done.3
  68.0 0.0 copy-done
  68.0 0.2 pad_maximum_fusion
  68.2 0.0 copy-start.2
  68.3 0.0 copy-start.3
  68.3 0.0 collective-permute-done.4
  68.3 0.0 collective-permute-done.5
  68.3 0.0 copy-done.1
  68.3 0.2 pad_maximum_fusion.1
  68.5 0.4 copy-done.2
  68.9 0.4 copy-done.3
  69.3 0.6 fusion.38
  69.9 0.6 fusion.39
  70.6 0.6 fusion.40
  71.2 0.6 fusion.41
  71.8 0.6 fusion.42
  72.5 2.3 %fusion.15 = (f32[384]{0:T(512)S(1)}, f32[384]{0:T(512)S(1)}, f32[384]{0:T(512)S(1)}, f32[384]{0:T(512)S(1)}, f32[384]{0:T(512)S(1)}) fusion(f32[384,1152]{0,1:T(8,128)S(1)} %get-tuple-element.11, f32[384]{0:T(512)S(1)} %get-tuple-element.10, s32[384]{0:T(512)S(1)} %copy-done.2, s32[1152]{0:T(1024)S(1)} %eq.38, pred[1152]{0:T(1024)(128)(4,1)S(1)} %and.30, ...), kind=kLoop, calls=%fused_computation.34 | loop fusion | flops 7518336 | bytes 8870016 | tf_op jit(solution)/shard_map/reduce_sum | solution.py:25
  74.8 0.9 constant_dynamic-update-slice_fusion.4
  75.7 0.9 constant_dynamic-update-slice_fusion.3
  76.6 0.9 constant_dynamic-update-slice_fusion.2
  77.6 0.9 constant_dynamic-update-slice_fusion.1
  78.5 0.9 constant_dynamic-update-slice_fusion
  79.4 0.1 collective-permute-start.6
  79.5 8.2 %collective-permute-done.6 = bf16[384,640]{0,1:T(8,128)(2,1)S(1)} collective-permute-done((bf16[384,640]{0,1:T(8,128)(2,1)S(1)}, bf16[384,640]{0,1:T(8,128)(2,1)S(1)}, u32[]{:S(2)}, u32[]{:S(2)}) %collective-permute-start.6) | collective-permute-done | bytes 491552 | tf_op jit(solution)/shard_map/ppermute | solution.py:87
  87.7 0.0 collective-permute-start.7
  87.7 8.3 %collective-permute-done.7 = bf16[384,640]{0,1:T(8,128)(2,1)S(1)} collective-permute-done((bf16[384,640]{0,1:T(8,128)(2,1)S(1)}, bf16[384,640]{0,1:T(8,128)(2,1)S(1)}, u32[]{:S(2)}, u32[]{:S(2)}) %collective-permute-start.7) | collective-permute-done | bytes 491552 | tf_op jit(solution)/shard_map/ppermute | solution.py:87
  96.0 0.0 collective-permute-start.8
  96.0 8.3 %collective-permute-done.8 = bf16[384,640]{0,1:T(8,128)(2,1)S(1)} collective-permute-done((bf16[384,640]{0,1:T(8,128)(2,1)S(1)}, bf16[384,640]{0,1:T(8,128)(2,1)S(1)}, u32[]{:S(2)}, u32[]{:S(2)}) %collective-permute-start.8) | collective-permute-done | bytes 491552 | tf_op jit(solution)/shard_map/ppermute | solution.py:87
  104.2 0.8 constant_dynamic-update-slice_fusion.20
  105.1 0.8 constant_dynamic-update-slice_fusion.19
  105.9 0.8 constant_dynamic-update-slice_fusion.18
  106.7 0.6 constant_dynamic-update-slice_fusion.17
  107.4 0.7 constant_dynamic-update-slice_fusion.16
  108.0 0.6 constant_dynamic-update-slice_fusion.15
  108.7 0.7 constant_dynamic-update-slice_fusion.14
  109.3 0.6 constant_dynamic-update-slice_fusion.13
  110.0 0.9 constant_dynamic-update-slice_fusion.12
  110.8 0.9 constant_dynamic-update-slice_fusion.11
  111.7 0.8 constant_dynamic-update-slice_fusion.10
  112.5 0.6 constant_dynamic-update-slice_fusion.9
  113.2 0.6 constant_dynamic-update-slice_fusion.8
  113.8 0.6 constant_dynamic-update-slice_fusion.7
  114.5 0.6 constant_dynamic-update-slice_fusion.6
  115.1 0.6 constant_dynamic-update-slice_fusion.5
  115.8 28.9 %all-gather.2.cloned.1.call-done = bf16[2560,1280]{1,0:T(8,128)(2,1)} async-done(((bf16[640,1280]{1,0:T(8,128)(2,1)}), bf16[2560,1280]{1,0:T(8,128)(2,1)}) %all-gather.2.cloned.1.call-update) | async-done | bytes 6553616 | tf_op jit(solution)/shard_map/all_gather | solution.py:93
  144.7 7.2 %convolution_convert_fusion = bf16[384,1280]{1,0:T(8,128)(2,1)} fusion(bf16[2560,1280]{1,0:T(8,128)(2,1)} %all-gather.2.cloned.1.call-done, bf16[384,5120]{0,1:T(8,128)(2,1)} %constant_dynamic-update-slice_fusion.5, s32[]{:T(128)S(6)} %select_n.60), kind=kOutput, calls=%fused_computation.15 | convolution fusion | flops 2517073920 | bytes 9502724 | tf_op jit(solution)/shard_map/dot_general | solution.py:95
  (6 shorter events, 0.1 us)
Async XLA Ops:
  6.5 61.5 %copy-start = (bf16[384,640]{1,0:T(8,128)(2,1)S(1)}, bf16[384,640]{1,0:T(8,128)(2,1)}, u32[]{:S(2)}) copy-start(bf16[384,640]{1,0:T(8,128)(2,1)} %param.8) | copy-start | bytes 1474564
  6.5 138.2 %all-gather.2.cloned.1.call-start = ((), (), s32[]{:S(2)}) async-start(), calls=%async_computation | async-start | bytes 8192000 | tf_op jit(solution)/shard_map/all_gather | solution.py:93
  7.3 61.0 %copy-start.1 = (bf16[384,640]{1,0:T(8,128)(2,1)S(1)}, bf16[384,640]{1,0:T(8,128)(2,1)}, u32[]{:S(2)}) copy-start(bf16[384,640]{1,0:T(8,128)(2,1)} %param.9) | copy-start | bytes 1474564
  7.3 60.8 %collective-permute-start.2 = (bf16[384,640]{1,0:T(8,128)(2,1)}, bf16[384,640]{1,0:T(8,128)(2,1)S(1)}, u32[]{:S(2)}, u32[]{:S(2)}) collective-permute-start(bf16[384,640]{1,0:T(8,128)(2,1)} %param.8), channel_id=1, source_target_pairs={{0,4},{4,8},{8,12},{1,5},{5,9},{9,13},{2,6},{6,10},{10,14},{3,7},{... | collective-permute-start | bytes 1474568 | tf_op jit(solution)/shard_map/ppermute | solution.py:15
  12.4 55.7 %collective-permute-start.3 = (bf16[384,640]{1,0:T(8,128)(2,1)}, bf16[384,640]{1,0:T(8,128)(2,1)S(1)}, u32[]{:S(2)}, u32[]{:S(2)}) collective-permute-start(bf16[384,640]{1,0:T(8,128)(2,1)} %param.8), channel_id=1, source_target_pairs={{4,0},{8,4},{12,8},{5,1},{9,5},{13,9},{6,2},{10,6},{14,10},{7,3},{... | collective-permute-start | bytes 1474568 | tf_op jit(solution)/shard_map/ppermute | solution.py:15
  13.7 54.6 %collective-permute-start.4 = (bf16[384,640]{1,0:T(8,128)(2,1)}, bf16[384,640]{1,0:T(8,128)(2,1)S(1)}, u32[]{:S(2)}, u32[]{:S(2)}) collective-permute-start(bf16[384,640]{1,0:T(8,128)(2,1)} %param.9), channel_id=1, source_target_pairs={{0,4},{4,8},{8,12},{1,5},{5,9},{9,13},{2,6},{6,10},{10,14},{3,7},{... | collective-permute-start | bytes 1474568 | tf_op jit(solution)/shard_map/ppermute | solution.py:15
  18.2 50.0 %collective-permute-start.5 = (bf16[384,640]{1,0:T(8,128)(2,1)}, bf16[384,640]{1,0:T(8,128)(2,1)S(1)}, u32[]{:S(2)}, u32[]{:S(2)}) collective-permute-start(bf16[384,640]{1,0:T(8,128)(2,1)} %param.9), channel_id=1, source_target_pairs={{4,0},{8,4},{12,8},{5,1},{9,5},{13,9},{6,2},{10,6},{14,10},{7,3},{... | collective-permute-start | bytes 1474568 | tf_op jit(solution)/shard_map/ppermute | solution.py:15
  19.5 27.6 %collective-permute-start = (s32[384]{0:T(512)}, s32[384]{0:T(512)S(1)}, u32[]{:S(2)}, u32[]{:S(2)}) collective-permute-start(s32[384]{0:T(512)} %param.12), channel_id=1, source_target_pairs={{0,4},{4,8},{8,12},{1,5},{5,9},{9,13},{2,6},{6,10},{10,14},{3,7},{... | collective-permute-start | bytes 4616 | tf_op jit(solution)/shard_map/ppermute | solution.py:15
  47.1 20.9 %collective-permute-start.1 = (s32[384]{0:T(512)}, s32[384]{0:T(512)S(1)}, u32[]{:S(2)}, u32[]{:S(2)}) collective-permute-start(s32[384]{0:T(512)} %param.12), channel_id=1, source_target_pairs={{4,0},{8,4},{12,8},{5,1},{9,5},{13,9},{6,2},{10,6},{14,10},{7,3},{... | collective-permute-start | bytes 4616 | tf_op jit(solution)/shard_map/ppermute | solution.py:15
  68.2 0.7 copy-start.2
  68.3 1.0 copy-start.3
  79.4 8.3 %collective-permute-start.6 = (bf16[384,640]{0,1:T(8,128)(2,1)S(1)}, bf16[384,640]{0,1:T(8,128)(2,1)S(1)}, u32[]{:S(2)}, u32[]{:S(2)}) collective-permute-start(bf16[384,640]{0,1:T(8,128)(2,1)S(1)} %get-tuple-element.28), channel_id=1, source_target_pairs={{0,1},{1,2},{2,3},{3,0},{4,5},{5,6},{6,7},{7,4},{8,9},{9,10},{10,1... | collective-permute-start | bytes 1474568 | tf_op jit(solution)/shard_map/ppermute | solution.py:87
  87.7 8.3 %collective-permute-start.7 = (bf16[384,640]{0,1:T(8,128)(2,1)S(1)}, bf16[384,640]{0,1:T(8,128)(2,1)S(1)}, u32[]{:S(2)}, u32[]{:S(2)}) collective-permute-start(bf16[384,640]{0,1:T(8,128)(2,1)S(1)} %collective-permute-done.6), channel_id=1, source_target_pairs={{0,1},{1,2},{2,3},{3,0},{4,5},{5,6},{6,7},{7,4},{8,9},{9,10},{10,1... | collective-permute-start | bytes 1474568 | tf_op jit(solution)/shard_map/ppermute | solution.py:87
  96.0 8.3 %collective-permute-start.8 = (bf16[384,640]{0,1:T(8,128)(2,1)S(1)}, bf16[384,640]{0,1:T(8,128)(2,1)S(1)}, u32[]{:S(2)}, u32[]{:S(2)}) collective-permute-start(bf16[384,640]{0,1:T(8,128)(2,1)S(1)} %collective-permute-done.7), channel_id=1, source_target_pairs={{0,1},{1,2},{2,3},{3,0},{4,5},{5,6},{6,7},{7,4},{8,9},{9,10},{10,1... | collective-permute-start | bytes 1474568 | tf_op jit(solution)/shard_map/ppermute | solution.py:87
Sparse Core Ops, SparseCore 0:
  8.9 135.7 all-gather.1
